TPU v7x, 256 devices: a whole 4x4x8 slice. The times are simulated.
256 devices in a mesh: row: 64 (over x, z_hi, y), col: 4 (over z_lo, core).
Axes of the slice: x: 4, y: 4, z: 8 (z_hi: 4, z_lo: 2; z = z_hi * 2 + z_lo), core: 2. Of those that a mesh axis runs over, the one named last changes fastest.
Arguments:
- img_hidden: bfloat16 [8, 1536, 2432], P(None, 'row', 'col'), may hold values from -6 to 6
- txt_hidden: bfloat16 [8, 128, 2432], P(None, 'row', 'col'), may hold values from -6 to 6
- latent: float32 [8, 1536, 64], P(None, 'row'), may hold values from -6 to 6
- img_mod: float32 [8, 5, 2432], replicated, may hold values from -4 to 4
- txt_mod: float32 [8, 2, 2432], replicated, may hold values from -4 to 4
- qkv_weight: bfloat16 [3, 2432, 2048], P(None, None, 'col'), may hold values from -0.125 to 0.125
- txt_kv_weight: bfloat16 [2, 2432, 2048], P(None, None, 'col'), may hold values from -0.125 to 0.125
- out_weight: bfloat16 [2048, 2432], P('col', 'row'), may hold values from -0.125 to 0.125
- final_weight: bfloat16 [2432, 64], P('col'), may hold values from -0.125 to 0.125
- qk_gains: float32 [3, 64], replicated, may hold values from 1.5 to 9
- txt_len: int32 [8], replicated, may hold values from 1 to 128, as said below
- step_idx: int32 [8], replicated, may hold values from 1 to 28
Outputs:
- advanced: float32 [8, 1536, 64], P(None, 'row')
- denoised: float32 [8, 1536, 64], P(None, 'row')
Inputs may be any that keep to these rules, and one draw needn't show every extreme that they name: `txt_len`: some request has all 128 text tokens live.
All inputs are finite; a program needn't handle non-finite values.
Results may differ from a plain program's by a relative error of at most 0.0044.
The roundings to bfloat16 on the way count: a program that leaves them out, or rounds other values in their place, can miss the bound.
Values may be sent and summed in bfloat16 or wider, within the bound.
No kernel may reach another device: no remote copies, remote signals or barrier semaphores. Data moves between devices by JAX's collectives and lax.ppermute only.
A program may use at most 128 MiB of HBM per device.

v0:
```python
import jax
import jax.numpy as jnp
from jax import lax
from jax.sharding import Mesh
from jax.sharding import PartitionSpec as P

D = 2432
HD = 64
STEPS = 28
REQ = 8
ROW = ("rq", "rm")
eps_norm = 1e-06
neg_fill = -1e30


def layer_norm(values):
    average = jnp.mean(values, -1, keepdims=True)
    centred = values - average
    variance = jnp.mean(centred * centred, -1, keepdims=True)
    return centred * lax.rsqrt(variance + eps_norm)


def rms_heads(values, scaling):
    reshaped = values.reshape(values.shape[:-1] + (values.shape[-1] // HD, HD))
    inverse = lax.rsqrt(jnp.mean(reshaped * reshaped, -1, keepdims=True) + eps_norm)
    return (reshaped * inverse * scaling).astype(jnp.bfloat16)


def sigma_at(indices):
    fraction = indices.astype(jnp.float32) / STEPS
    return 3.0 * fraction / (1.0 + 2.0 * fraction)


def gather_features(local):
    stacked = lax.all_gather(local, "col", axis=0, tiled=False)
    slabs = stacked.shape[0]
    moved = jnp.moveaxis(stacked, 0, -2)
    return moved.reshape(local.shape[:-1] + (slabs * local.shape[-1],))


def attend_one(queries, keys, values, allowed):
    scores = jnp.einsum("qhd,khd->hqk", queries, keys, preferred_element_type=jnp.float32) * HD ** (
        -0.5
    )
    scores = jnp.where(allowed[None, None, :], scores, neg_fill)
    top_score = jnp.max(scores, -1, keepdims=True)
    exp_scores = jnp.where(allowed[None, None, :], jnp.exp(scores - top_score), 0.0)
    row_total = jnp.sum(exp_scores, -1)
    weighted = jnp.einsum(
        "hqk,khd->qhd", exp_scores.astype(jnp.bfloat16), values, preferred_element_type=jnp.float32
    )
    return (weighted / jnp.transpose(row_total)[..., None]).astype(jnp.bfloat16)


def per_device(
    img_hidden,
    txt_hidden,
    latent,
    img_mod,
    txt_mod,
    qkv_weight,
    txt_kv_weight,
    out_weight,
    final_weight,
    qk_gains,
    txt_len,
    step_idx,
):
    requests = img_hidden.shape[0]
    patches = img_hidden.shape[1]
    text_rows = txt_hidden.shape[1]
    cols_local = qkv_weight.shape[2]
    heads_local = cols_local // HD
    block_len = patches + text_rows
    groups = lax.axis_size("rq")
    members = lax.axis_size("rm")
    weight_t = lax.all_gather(jnp.transpose(out_weight), ROW, axis=0, tiled=True)
    img_full = gather_features(img_hidden)
    txt_full = gather_features(txt_hidden)
    img_wide = img_full.astype(jnp.float32)
    normed = (layer_norm(img_wide) * (1.0 + img_mod[:, 1:2, :]) + img_mod[:, 0:1, :]).astype(
        jnp.bfloat16
    )
    flat_rows = normed.reshape(requests * patches, D)
    projected = jnp.einsum("td,cde->cte", flat_rows, qkv_weight, preferred_element_type=jnp.float32)
    queries = rms_heads(projected[0], qk_gains[0]).reshape(requests, patches, cols_local)
    img_keys = rms_heads(projected[1], qk_gains[1]).reshape(requests, patches, cols_local)
    img_values = projected[2].astype(jnp.bfloat16).reshape(requests, patches, cols_local)
    text_normed = (
        layer_norm(txt_full.astype(jnp.float32)) * (1.0 + txt_mod[:, 1:2, :]) + txt_mod[:, 0:1, :]
    ).astype(jnp.bfloat16)
    text_proj = jnp.einsum(
        "rtd,cde->crte", text_normed, txt_kv_weight, preferred_element_type=jnp.float32
    )
    text_keys = rms_heads(text_proj[0], qk_gains[2]).reshape(requests, text_rows, cols_local)
    text_values = text_proj[1].astype(jnp.bfloat16)
    key_rows = jnp.concatenate([img_keys, text_keys], 1)
    value_rows = jnp.concatenate([img_values, text_values], 1)
    kv_rows = jnp.stack([key_rows, value_rows], 1)
    group_queries = lax.all_to_all(queries, "rq", 0, 0, tiled=True)
    group_kv = lax.all_to_all(kv_rows, "rq", 0, 0, tiled=True)
    all_kv = lax.all_gather(group_kv, "rm", axis=0, tiled=False)
    key_count = members * groups * block_len
    keys = all_kv[:, :, 0].reshape(key_count, heads_local, HD)
    values = all_kv[:, :, 1].reshape(key_count, heads_local, HD)
    request = lax.axis_index("rq")
    positions = jnp.arange(key_count, dtype=jnp.int32)
    within = positions % block_len
    source_block = positions // block_len
    member_of = source_block // groups
    group_of = source_block % groups
    source_row = group_of * members + member_of
    text_pos = source_row * text_rows + within - patches
    live_text = text_pos < lax.dynamic_index_in_dim(txt_len, request, keepdims=False)
    allowed = (within < patches) | live_text
    attended = attend_one(
        group_queries.reshape(groups * patches, heads_local, HD), keys, values, allowed
    ).reshape(groups, patches, cols_local)
    attended = lax.all_to_all(attended, "rq", 0, 0, tiled=True).reshape(
        requests * patches, cols_local
    )
    partial_value = lax.dot_general(
        attended, weight_t, (((1,), (1,)), ((), ())), preferred_element_type=jnp.float32
    )
    slab_width = img_hidden.shape[2]
    col_index = lax.axis_index("col")
    shared_sum = lax.psum_scatter(partial_value, "col", scatter_dimension=1, tiled=True)
    col_mods = lax.dynamic_slice_in_dim(img_mod, col_index * slab_width, slab_width, 2)
    mixed = img_hidden.astype(jnp.float32) + col_mods[:, 2:3, :] * shared_sum.reshape(
        requests, patches, slab_width
    )
    row_sums, squares = lax.psum((jnp.sum(mixed, -1), jnp.sum(mixed * mixed, -1)), "col")
    row_mean = row_sums / D
    spread = squares / D - row_mean * row_mean
    scaled = (mixed - row_mean[..., None]) * lax.rsqrt(spread[..., None] + eps_norm)
    modulated = (scaled * (1.0 + col_mods[:, 4:5, :]) + col_mods[:, 3:4, :]).astype(jnp.bfloat16)
    velocity = lax.psum(
        jnp.dot(
            modulated.reshape(requests * patches, slab_width),
            final_weight,
            preferred_element_type=jnp.float32,
        ),
        "col",
    )
    velocity = velocity.reshape(requests, patches, latent.shape[2])
    sigma_now = sigma_at(step_idx)[:, None, None]
    sigma_next = sigma_at(step_idx - 1)[:, None, None]
    advanced = latent + (sigma_next - sigma_now) * velocity
    denoised = latent - sigma_now * velocity
    return (advanced, denoised)


def solution(mesh):
    rows = mesh.shape["row"]
    cols = mesh.shape["col"]
    split = Mesh(mesh.devices.reshape(REQ, rows // REQ, cols), ("rq", "rm", "col"))
    in_specs = (
        P(None, ROW, "col"),
        P(None, ROW, "col"),
        P(None, ROW, None),
        P(),
        P(),
        P(None, None, "col"),
        P(None, None, "col"),
        P("col", ROW),
        P("col", None),
        P(),
        P(),
        P(),
    )
    out_specs = (P(None, ROW, None), P(None, ROW, None))
    return jax.shard_map(
        per_device, mesh=split, in_specs=in_specs, out_specs=out_specs, check_vma=False
    )
```

profile of v0, /device:TPU:1, one launch (start us, length us, event | category | flops | bytes accessed | tf_op | source)
XLA Modules:
  0.0 299.0 jit_solution(12010077146269406684)
XLA Ops:
  7.2 8.6 %all-gather.1 = bf16[32,2,608]{2,1,0:T(2,128)(2,1)S(1)} all-gather(bf16[8,2,608]{2,1,0:T(2,128)(2,1)} %param.13), channel_id=3, replica_groups=mesh['rq'=8,'rm'=8,'col'=4] {'col'}, dimensions={0}, use_global_device_ids=true | all-gather | bytes 97280 | tf_op jit(solution)/shard_map/all_gather | solution.py:35
  15.9 0.2 fusion.65
  16.1 10.0 %all-gather = bf16[32,24,608]{2,1,0:T(8,128)(2,1)S(1)} all-gather(bf16[8,24,608]{2,1,0:T(8,128)(2,1)} %param.12), channel_id=2, replica_groups=mesh['rq'=8,'rm'=8,'col'=4] {'col'}, dimensions={0}, use_global_device_ids=true | all-gather | bytes 1167360 | tf_op jit(solution)/shard_map/all_gather | solution.py:35
  26.1 0.2 fusion.31
  26.4 0.4 multiply_reduce_fusion
  27.2 0.3 multiply_reduce_fusion.2
  27.9 3.2 %fusion.28 = f32[2,8,2,512]{3,1,0,2:T(8,128)S(1)} fusion(bf16[2,2432,512]{2,1,0:T(8,128)(2,1)} %param.18, f32[8,2,2432]{2,0,1:T(8,128)S(1)} %reshape.182, f32[8,2432]{1,0:T(8,128)S(1)} %get-tuple-element.30, f32[8,2432]{1,0:T(8,128)S(1)} %get-tuple-element.31, f32[8,2]{0,1:T(2,128)S(1)} %copy.88, f32[8,2]{0,1:T(2,128)S(1)} %copy.85), kind=kOutput, calls=%fused_computation.26 | convolution fusion | flops 79886336 | bytes 5357696 | tf_op jit(solution)/shard_map/rtd,cde->crte/dot_general | solution.py:92
  31.2 2.6 copy.80
  33.8 2.2 reshape.181
  36.0 0.9 add_bitcast_fusion
  37.0 0.5 fusion.12
  37.5 4.8 %convolution_bitcast_fusion.1 = f32[3,192,512]{2,1,0:T(8,128)S(1)} fusion(bf16[3,2432,512]{2,1,0:T(8,128)(2,1)} %param.17, bf16[192,2432]{1,0:T(8,128)(2,1)S(1)} %fusion.12), kind=kOutput, calls=%fused_computation.22 | convolution fusion | flops 1434451968 | bytes 9584640 | tf_op jit(solution)/shard_map/td,cde->cte/dot_general | solution.py:85
  43.0 0.2 copy.81
  43.4 0.3 mul.268
  43.6 0.2 mul.269
  44.2 0.4 copy.93
  44.6 21.4 %all_to_all.15 = bf16[8,2,26,512]{3,1,2,0:T(2,128)(2,1)} all-to-all(bf16[8,2,26,512]{3,1,2,0:T(2,128)(2,1)S(1)} %copy.93), channel_id=1, replica_groups=mesh['rq'=8,'rm'=8,'col'=4] {'rq'}, dimensions={0} | all-to-all | bytes 851968 | tf_op jit(solution)/shard_map/all_to_all | solution.py:101
  66.2 0.7 all-gather.9.cloned.1.call-update
  66.9 0.2 copy.95
  67.2 0.3 mul.297
  67.5 0.2 mul.298
  67.8 0.7 multiply_convert_fusion
  68.6 3.6 %all-to-all-start.1 = ((bf16[8,24,512]{2,1,0:T(8,128)(2,1)}), bf16[8,24,512]{2,1,0:T(8,128)(2,1)S(1)}, u32[]{:S(2)}, u32[]{:S(2)}) async-start(bf16[8,24,512]{2,1,0:T(8,128)(2,1)} %multiply_convert_fusion), calls=%async_computation.1 | async-start | bytes 393216 | tf_op jit(solution)/shard_map/all_to_all | solution.py:100
  72.2 0.6 dynamic_slice.8
  72.7 0.7 fusion.60
  73.4 8.2 %all-to-all-done.1 = bf16[8,24,512]{2,1,0:T(8,128)(2,1)S(1)} async-done(((bf16[8,24,512]{2,1,0:T(8,128)(2,1)}), bf16[8,24,512]{2,1,0:T(8,128)(2,1)S(1)}, u32[]{:S(2)}, u32[]{:S(2)}) %all-to-all-start.1) | async-done | bytes 196640 | tf_op jit(solution)/shard_map/all_to_all | solution.py:100
  81.6 1.0 reshape.175
  82.6 66.5 %all-gather.7.cloned.1.call-done = bf16[64,2,26,512]{3,1,2,0:T(2,128)(2,1)} async-done(((bf16[8,2,26,512]{3,1,2,0:T(2,128)(2,1)}), bf16[64,2,26,512]{3,1,2,0:T(2,128)(2,1)}) %all-gather.7.cloned.1.call-update) | async-done | bytes 3407888 | tf_op jit(solution)/shard_map/all_gather | solution.py:102
  149.1 25.3 %slice_reduce_fusion.1 = (bf16[8,8,26,512]{3,2,1,0:T(8,128)(2,1)}, bf16[8,8,26,512]{3,2,1,0:T(8,128)(2,1)}) fusion(bf16[8,8,2,26,512]{4,2,3,1,0:T(2,128)(2,1)} %bitcast.118), kind=kLoop, calls=%fused_computation.13 | loop fusion | bytes 6815744 | tf_op jit(solution)/shard_map/slice | solution.py:105
  174.5 4.3 %reshape_squeeze.19 = bf16[1664,8,64]{2,1,0:T(8,128)(2,1)S(1)} reshape(bf16[8,8,26,512]{3,2,1,0:T(8,128)(2,1)} %get-tuple-element.3) | data formatting | bytes 3407872 | tf_op jit(solution)/shard_map/reshape;squeeze | solution.py:104
  178.8 5.7 %reshape_squeeze.17 = bf16[1664,8,64]{2,1,0:T(8,128)(2,1)} reshape(bf16[8,8,26,512]{3,2,1,0:T(8,128)(2,1)} %get-tuple-element.2) | data formatting | bytes 3407872 | tf_op jit(solution)/shard_map/reshape;squeeze | solution.py:105
  184.4 6.4 %fusion.10 = f32[8,192,1664]{2,1,0:T(8,128)} fusion(bf16[1664,8,64]{2,1,0:T(8,128)(2,1)S(1)} %reshape_squeeze.19, bf16[192,8,64]{2,1,0:T(8,128)(2,1)} %reshape.175), kind=kOutput, calls=%fused_computation.15 | convolution fusion | flops 327155712 | bytes 12124160 | tf_op jit(solution)/shard_map/qhd,khd->hqk/dot_general | solution.py:42
  190.9 12.9 %fusion.67 = (f32[8,192]{1,0:T(8,128)S(1)}, bf16[8,192,1664]{2,1,0:T(8,128)(2,1)}) fusion(f32[8,192,1664]{2,1,0:T(8,128)} %fusion.10, pred[1664]{0:T(1024)(128)(4,1)S(1)} %fusion.60), kind=kOutput, calls=%fused_computation.113 | output fusion | flops 20448896 | bytes 15343232 | tf_op jit(solution)/shard_map/sub | solution.py:47
  203.8 4.4 %fusion.23 = bf16[192,8,64]{0,2,1:T(8,128)(2,1)S(1)} fusion(bf16[8,192,1664]{2,1,0:T(8,128)(2,1)} %get-tuple-element.29, bf16[1664,8,64]{2,1,0:T(8,128)(2,1)S(1)} %copy-done.1, f32[192,8]{0,1:T(8,128)S(1)} %bitcast.132), kind=kOutput, calls=%fused_computation.25 | convolution fusion | flops 327352320 | bytes 7018496 | tf_op jit(solution)/shard_map/hqk,khd->qhd/dot_general | solution.py:49
  208.2 0.2 copy.101
  208.5 0.9 reshape.176
  209.4 7.7 %all-to-all-start.2 = ((bf16[8,24,512]{2,1,0:T(8,128)(2,1)}), bf16[8,24,512]{2,1,0:T(8,128)(2,1)S(1)}, u32[]{:S(2)}, u32[]{:S(2)}) async-start(bf16[8,24,512]{2,1,0:T(8,128)(2,1)} %reshape.176), calls=%async_computation.2 | async-start | bytes 393216 | tf_op jit(solution)/shard_map/all_to_all | solution.py:119
  217.1 15.6 %all-gather.9.cloned.1.call-done = bf16[64,38,512]{2,1,0:T(8,128)(2,1)} async-done(((bf16[1,38,512]{2,1,0:T(8,128)(2,1)}), bf16[64,38,512]{2,1,0:T(8,128)(2,1)}) %all-gather.9.cloned.1.call-update) | async-done | bytes 2490384 | tf_op jit(solution)/shard_map/all_gather | solution.py:77
  232.7 2.8 reshape.191
  235.5 2.3 convolution_bitcast_fusion
  237.8 0.9 dynamic-slice_bitcast_fusion.1
  238.7 34.1 %reduce-scatter.4.cloned.1.call-done = f32[608,192]{1,0:T(8,128)} async-done(((f32[2432,192]{1,0:T(8,128)}), f32[608,192]{1,0:T(8,128)}) %reduce-scatter.4.cloned.1.call-update) | async-done | bytes 466960
  272.9 1.3 copy.106
  274.3 5.5 %all-reduce = (f32[8,24]{1,0:T(8,128)S(1)}, f32[8,24]{1,0:T(8,128)S(1)}) all-reduce(f32[8,24]{1,0:T(8,128)S(1)} %get-tuple-element.5, f32[8,24]{1,0:T(8,128)S(1)} %get-tuple-element.4), channel_id=1, replica_groups=mesh['rq'=8,'rm'=8,'col'=4] {'col'}, use_global_device_ids=true, to_apply=%region_13.14 | all-reduce | flops 384 | bytes 3072 | tf_op jit(solution)/shard_map/psum | solution.py:132
  279.9 0.2 add_convert_fusion
  280.1 0.2 fusion.68
  280.3 11.4 %psum.23 = f32[8,24,64]{2,1,0:T(8,128)S(1)} all-reduce(f32[8,24,64]{2,1,0:T(8,128)S(1)} %bitcast.130), channel_id=1, replica_groups=mesh['rq'=8,'rm'=8,'col'=4] {'col'}, use_global_device_ids=true, to_apply=%region_14.15 | all-reduce | flops 12288 | bytes 98304 | tf_op jit(solution)/shard_map/psum | solution.py:137
  291.8 0.8 multiply_subtract_fusion
  (70 shorter events, 2.8 us)
Async XLA Ops:
  7.2 272.9 %copy-start = (bf16[608,64]{0,1:T(8,128)(2,1)S(1)}, bf16[608,64]{0,1:T(8,128)(2,1)}, u32[]{:S(2)}) copy-start(bf16[608,64]{0,1:T(8,128)(2,1)} %param.20) | copy-start | bytes 233476
  7.2 141.9 %all-gather.7.cloned.1.call-start = ((), (), s32[]{:S(2)}) async-start(), calls=%async_computation.4 | async-start | bytes 3833856 | tf_op jit(solution)/shard_map/all_gather | solution.py:102
  15.9 11.8 %copy-start.3 = (f32[8,2,2432]{2,1,0:T(2,128)S(1)}, f32[8,2,2432]{2,1,0:T(2,128)}, u32[]{:S(2)}) copy-start(f32[8,2,2432]{2,1,0:T(2,128)} %param.16) | copy-start | bytes 466948
  37.4 5.4 %copy-start.5 = (f32[3,64]{1,0:T(4,128)S(1)}, f32[3,64]{1,0:T(4,128)}, u32[]{:S(2)}) copy-start(f32[3,64]{1,0:T(4,128)} %param.21) | copy-start | bytes 2308
  44.6 27.5 %copy-start.6 = (s32[8]{0:T(128)S(1)}, s32[8]{0:T(128)}, u32[]{:S(2)}) copy-start(s32[8]{0:T(128)} %param.22) | copy-start | bytes 100
  66.1 166.6 %all-gather.9.cloned.1.call-start = ((), (), s32[]{:S(2)}) async-start(), calls=%async_computation.5 | async-start | bytes 2662400 | tf_op jit(solution)/shard_map/all_gather | solution.py:77
  68.6 13.0 %all-to-all-start.1 = ((bf16[8,24,512]{2,1,0:T(8,128)(2,1)}), bf16[8,24,512]{2,1,0:T(8,128)(2,1)S(1)}, u32[]{:S(2)}, u32[]{:S(2)}) async-start(bf16[8,24,512]{2,1,0:T(8,128)(2,1)} %multiply_convert_fusion), calls=%async_computation.1 | async-start | bytes 393216 | tf_op jit(solution)/shard_map/all_to_all | solution.py:100
  190.9 12.9 %copy-start.1 = (bf16[1664,8,64]{2,1,0:T(8,128)(2,1)S(1)}, bf16[1664,8,64]{2,1,0:T(8,128)(2,1)}, u32[]{:S(2)}) copy-start(bf16[1664,8,64]{2,1,0:T(8,128)(2,1)} %reshape_squeeze.17) | copy-start | bytes 5111812
  209.4 26.1 %all-to-all-start.2 = ((bf16[8,24,512]{2,1,0:T(8,128)(2,1)}), bf16[8,24,512]{2,1,0:T(8,128)(2,1)S(1)}, u32[]{:S(2)}, u32[]{:S(2)}) async-start(bf16[8,24,512]{2,1,0:T(8,128)(2,1)} %reshape.176), calls=%async_computation.2 | async-start | bytes 393216 | tf_op jit(solution)/shard_map/all_to_all | solution.py:119
  217.1 55.8 %reduce-scatter.4.cloned.1.call-start = ((), (), s32[]{:S(2)}) async-start(), calls=%async_computation.6 | async-start | bytes 3112960
  235.5 3.2 %copy-start.7 = (s32[8]{0:T(128)S(1)}, s32[8]{0:T(128)}, u32[]{:S(2)}) copy-start(s32[8]{0:T(128)} %param.23) | copy-start | bytes 100
  237.7 36.4 %copy-start.2 = (bf16[8,24,608]{2,1,0:T(8,128)(2,1)S(1)}, bf16[8,24,608]{2,1,0:T(8,128)(2,1)}, u32[]{:S(2)}) copy-start(bf16[8,24,608]{2,1,0:T(8,128)(2,1)} %param.12) | copy-start | bytes 700420
  237.7 54.0 %copy-start.4 = (f32[8,24,64]{2,1,0:T(8,128)S(1)}, f32[8,24,64]{2,1,0:T(8,128)}, u32[]{:S(2)}) copy-start(f32[8,24,64]{2,1,0:T(8,128)} %param.14) | copy-start | bytes 147460
Sparse Core Ops, SparseCore 0:
  66.2 82.8 all-gather.6
  152.4 80.2 all-gather.8
  237.9 34.9 reduce-scatter.3
where the time goes:
time: 300 us; the launch traced here: 299 us
  waiting for transfers between devices  125 us (42%)
  blocking collectives  57 us (19%)
  local copies, waits for them, and re-layouts  50.3 us (17%)
  matrix products  21.3 us (7%)
  other arithmetic  19.7 us (7%)
  between operations  14.2 us (5%)
  starting transfers between devices  11.3 us (4%)
    all_gather x1, waiting for transfers between devices, per_device(): all_kv = lax.all_gather(group_kv, 'rm', axis=0, tiled=False)  66.5 us
    unnamed x4, waiting for transfers between devices  34.8 us
    slice x1, local copies, waits for them, and re-layouts, per_device(): values = all_kv[:, :, 1].reshape(key_count, heads_local, HD)  25.3 us
    all_to_all x1, blocking collectives, per_device(): group_kv = lax.all_to_all(kv_rows, 'rq', 0, 0, tiled=True)  21.4 us
    all_gather x2, blocking collectives, gather_features(): stacked = lax.all_gather(local, 'col', axis=0, tiled=False)  18.6 us
    all_gather x1, waiting for transfers between devices, per_device(): lax.all_gather(jnp.transpose(out_weight), ROW, axis=0, tiled=True)  15.6 us
    sub x1, other arithmetic, attend_one(): scores - top_score  12.9 us
    psum x1, blocking collectives, per_device(): lax.psum(jnp.dot(modulated.reshape(requests * patches, slab_width), final...  11.4 us
  transfers between devices with their start and end apart: 5, of which 4 were waited for; matrix products, arithmetic and copies ran while one was open for 23% of the time, Pallas kernels for 0%

commit v1 on v0

--- a/solution.py
+++ b/solution.py
@@ -1,8 +1,10 @@
+import functools
 import jax
 import jax.numpy as jnp
 from jax import lax
 from jax.sharding import Mesh
 from jax.sharding import PartitionSpec as P
+from jax.lax import all_to_all, psum
 
 D = 2432
 HD = 64
@@ -11,6 +13,18 @@
 ROW = ("rq", "rm")
 eps_norm = 1e-06
 neg_fill = -1e30
+
+
+def follow_the_pieces_all(work_x, row_axis):
+    grid = []
+    for _ in range(psum(1, row_axis)):
+        grid.append(work_x)
+    return jnp.concatenate(
+        all_to_all(jnp.stack(grid, axis=0), row_axis, concat_axis=0, split_axis=0), axis=0
+    )
+
+
+group_shapes = functools.partial(follow_the_pieces_all, row_axis=ROW)
 
 
 def layer_norm(values):
@@ -74,7 +88,7 @@
     block_len = patches + text_rows
     groups = lax.axis_size("rq")
     members = lax.axis_size("rm")
-    weight_t = lax.all_gather(jnp.transpose(out_weight), ROW, axis=0, tiled=True)
+    weight_t = group_shapes(jnp.transpose(out_weight))
     img_full = gather_features(img_hidden)
     txt_full = gather_features(txt_hidden)
     img_wide = img_full.astype(jnp.float32)

time: 300 us -> 342 us (1.14)
  waiting for transfers between devices: 125 us -> 146 us
  blocking collectives: 57 us -> 69.1 us
  starting transfers between devices: 11.3 us -> 18.7 us
    all_gather x1, waiting for transfers between devices: 66.5 us -> 109 us  [per_device(): all_kv = lax.all_gather(group_kv, 'rm', axis=0, tiled=False)]
    all_gather x1 -> x0, waiting for transfers between devices: 15.6 us -> none  [per_device(): lax.all_gather(jnp.transpose(out_weight), ROW, axis=0, tiled=True)]
    all_to_all x0 -> x1, blocking collectives: none -> 12.1 us  [per_device(): group_queries = lax.all_to_all(queries, 'rq', 0, 0, tiled=True)]
    all_to_all x1, starting transfers between devices: 3.57 us -> 12.8 us  [follow_the_pieces_all(): all_to_all(jnp.stack(grid, axis=0), row_axis, concat_axis=0, split_axis=0)]
    all_to_all x1, waiting for transfers between devices: 8.19 us -> 0.01 us  [follow_the_pieces_all(): all_to_all(jnp.stack(grid, axis=0), row_axis, concat_axis=0, split_axis=0)]
    all_to_all x1, waiting for transfers between devices: 0.01 us -> 6.89 us  [per_device(): lax.all_to_all(attended, 'rq', 0, 0, tiled=True)]
    unnamed x4 -> x3, waiting for transfers between devices: 34.8 us -> 29.9 us
  transfers between devices with their start and end apart: 5 -> 4, of which waited for: 4 -> 3; matrix products, arithmetic and copies ran while one was open for 23% -> 20% of each run, Pallas kernels for 0% -> 0%
where the time goes in v1:
time: 342 us; the launch traced here: 341 us
  waiting for transfers between devices  146 us (43%)
  blocking collectives  69.1 us (20%)
  local copies, waits for them, and re-layouts  52 us (15%)
  matrix products  21.3 us (6%)
  other arithmetic  18.9 us (6%)
  starting transfers between devices  18.7 us (5%)
  between operations  14.5 us (4%)
    all_gather x1, waiting for transfers between devices, per_device(): all_kv = lax.all_gather(group_kv, 'rm', axis=0, tiled=False)  109 us
    unnamed x3, waiting for transfers between devices  29.9 us
    slice x1, local copies, waits for them, and re-layouts, per_device(): values = all_kv[:, :, 1].reshape(key_count, heads_local, HD)  25.3 us
    all_to_all x1, blocking collectives, per_device(): group_kv = lax.all_to_all(kv_rows, 'rq', 0, 0, tiled=True)  21.4 us
    all_gather x2, blocking collectives, gather_features(): stacked = lax.all_gather(local, 'col', axis=0, tiled=False)  18.6 us
    sub x1, other arithmetic, attend_one(): scores - top_score  12.8 us
    all_to_all x1, starting transfers between devices, follow_the_pieces_all(): all_to_all(jnp.stack(grid, axis=0), row_axis, concat_axis=0, split_axis=0)  12.8 us
    all_to_all x1, blocking collectives, per_device(): group_queries = lax.all_to_all(queries, 'rq', 0, 0, tiled=True)  12.1 us
  transfers between devices with their start and end apart: 4, of which 3 were waited for; matrix products, arithmetic and copies ran while one was open for 20% of the time, Pallas kernels for 0%

profile of v1, /device:TPU:1, one launch (start us, length us, event | category | flops | bytes accessed | tf_op | source)
XLA Modules:
  0.0 340.6 jit_solution(3948090975154213054)
XLA Ops:
  7.2 8.6 %all-gather.1 = bf16[32,2,608]{2,1,0:T(2,128)(2,1)S(1)} all-gather(bf16[8,2,608]{2,1,0:T(2,128)(2,1)} %param.13), channel_id=3, replica_groups=mesh['rq'=8,'rm'=8,'col'=4] {'col'}, dimensions={0}, use_global_device_ids=true | all-gather | bytes 97280 | tf_op jit(solution)/shard_map/all_gather | solution.py:49
  15.9 0.2 fusion.65
  16.1 10.0 %all-gather = bf16[32,24,608]{2,1,0:T(8,128)(2,1)S(1)} all-gather(bf16[8,24,608]{2,1,0:T(8,128)(2,1)} %param.12), channel_id=2, replica_groups=mesh['rq'=8,'rm'=8,'col'=4] {'col'}, dimensions={0}, use_global_device_ids=true | all-gather | bytes 1167360 | tf_op jit(solution)/shard_map/all_gather | solution.py:49
  26.1 0.2 fusion.31
  26.4 0.4 multiply_reduce_fusion
  27.2 0.3 multiply_reduce_fusion.2
  27.9 3.2 fusion.28
  31.2 2.6 copy.80
  33.8 2.2 reshape.187
  36.0 0.9 add_bitcast_fusion
  37.0 0.5 fusion.12
  37.5 4.8 %convolution_bitcast_fusion.1 = f32[3,192,512]{2,1,0:T(8,128)S(1)} fusion(bf16[3,2432,512]{2,1,0:T(8,128)(2,1)} %param.17, bf16[192,2432]{1,0:T(8,128)(2,1)S(1)} %fusion.12), kind=kOutput, calls=%fused_computation.22 | convolution fusion | flops 1434451968 | bytes 9584640 | tf_op jit(solution)/shard_map/td,cde->cte/dot_general | solution.py:99
  42.3 0.2 slice_multiply_fusion.1
  43.0 0.2 copy.81
  43.4 0.3 mul.268
  43.6 0.2 mul.269
  44.2 0.4 copy.93
  44.6 21.4 %all_to_all.20 = bf16[8,2,26,512]{3,1,2,0:T(2,128)(2,1)} all-to-all(bf16[8,2,26,512]{3,1,2,0:T(2,128)(2,1)S(1)} %copy.93), channel_id=1, replica_groups=mesh['rq'=8,'rm'=8,'col'=4] {'rq'}, dimensions={0} | all-to-all | bytes 851968 | tf_op jit(solution)/shard_map/all_to_all | solution.py:115
  66.1 0.2 copy.95
  66.5 0.3 mul.297
  66.7 0.2 mul.298
  67.1 12.1 %all_to_all.21 = bf16[8,24,512]{2,1,0:T(8,128)(2,1)S(1)} all-to-all(bf16[8,24,512]{2,1,0:T(8,128)(2,1)S(1)} %multiply_convert_fusion), channel_id=1, replica_groups=mesh['rq'=8,'rm'=8,'col'=4] {'rq'}, dimensions={0} | all-to-all | bytes 393216 | tf_op jit(solution)/shard_map/all_to_all | solution.py:114
  79.3 1.7 stack.11
  80.9 12.8 %all-to-all-start.3 = ((bf16[64,38,512]{2,1,0:T(8,128)(2,1)}), bf16[64,38,512]{2,1,0:T(8,128)(2,1)}, u32[]{:S(2)}, u32[]{:S(2)}) async-start(bf16[64,38,512]{2,1,0:T(8,128)(2,1)} %stack.11), calls=%async_computation.3 | async-start | bytes 5242880 | tf_op jit(solution)/shard_map/all_to_all | solution.py:23
  93.8 0.6 dynamic_slice.8
  94.4 0.7 fusion.60
  95.0 1.0 reshape.180
  96.0 109.2 %all-gather.5.cloned.1.call-done = bf16[64,2,26,512]{3,1,2,0:T(2,128)(2,1)} async-done(((bf16[8,2,26,512]{3,1,2,0:T(2,128)(2,1)}), bf16[64,2,26,512]{3,1,2,0:T(2,128)(2,1)}) %all-gather.5.cloned.1.call-update) | async-done | bytes 3407888 | tf_op jit(solution)/shard_map/all_gather | solution.py:116
  205.3 25.3 %slice_reduce_fusion.1 = (bf16[8,8,26,512]{3,2,1,0:T(8,128)(2,1)}, bf16[8,8,26,512]{3,2,1,0:T(8,128)(2,1)}) fusion(bf16[8,8,2,26,512]{4,2,3,1,0:T(2,128)(2,1)} %bitcast.116), kind=kLoop, calls=%fused_computation.13 | loop fusion | bytes 6815744 | tf_op jit(solution)/shard_map/slice | solution.py:119
  230.6 4.3 %reshape_squeeze.19 = bf16[1664,8,64]{2,1,0:T(8,128)(2,1)S(1)} reshape(bf16[8,8,26,512]{3,2,1,0:T(8,128)(2,1)} %get-tuple-element.3) | data formatting | bytes 3407872 | tf_op jit(solution)/shard_map/reshape;squeeze | solution.py:118
  234.9 5.7 %reshape_squeeze.17 = bf16[1664,8,64]{2,1,0:T(8,128)(2,1)} reshape(bf16[8,8,26,512]{3,2,1,0:T(8,128)(2,1)} %get-tuple-element.2) | data formatting | bytes 3407872 | tf_op jit(solution)/shard_map/reshape;squeeze | solution.py:119
  240.6 6.4 %fusion.10 = f32[8,192,1664]{2,1,0:T(8,128)} fusion(bf16[1664,8,64]{2,1,0:T(8,128)(2,1)S(1)} %reshape_squeeze.19, bf16[192,8,64]{2,1,0:T(8,128)(2,1)} %reshape.180), kind=kOutput, calls=%fused_computation.15 | convolution fusion | flops 327155712 | bytes 12124160 | tf_op jit(solution)/shard_map/qhd,khd->hqk/dot_general | solution.py:56
  247.0 12.8 %fusion.67 = (f32[8,192]{1,0:T(8,128)S(1)}, bf16[8,192,1664]{2,1,0:T(8,128)(2,1)}) fusion(f32[8,192,1664]{2,1,0:T(8,128)} %fusion.10, pred[1664]{0:T(1024)(128)(4,1)S(1)} %fusion.60), kind=kOutput, calls=%fused_computation.113 | output fusion | flops 20448896 | bytes 15343232 | tf_op jit(solution)/shard_map/sub | solution.py:61
  259.8 4.4 %fusion.23 = bf16[192,8,64]{0,2,1:T(8,128)(2,1)S(1)} fusion(bf16[8,192,1664]{2,1,0:T(8,128)(2,1)} %get-tuple-element.29, bf16[1664,8,64]{2,1,0:T(8,128)(2,1)S(1)} %copy-done.1, f32[192,8]{0,1:T(8,128)S(1)} %bitcast.130), kind=kOutput, calls=%fused_computation.25 | convolution fusion | flops 327352320 | bytes 7018496 | tf_op jit(solution)/shard_map/hqk,khd->qhd/dot_general | solution.py:63
  264.2 0.2 copy.101
  264.5 0.9 reshape.181
  265.4 5.8 %all-to-all-start.2 = ((bf16[8,24,512]{2,1,0:T(8,128)(2,1)}), bf16[8,24,512]{2,1,0:T(8,128)(2,1)S(1)}, u32[]{:S(2)}, u32[]{:S(2)}) async-start(bf16[8,24,512]{2,1,0:T(8,128)(2,1)} %reshape.181), calls=%async_computation.2 | async-start | bytes 393216 | tf_op jit(solution)/shard_map/all_to_all | solution.py:133
  271.3 2.8 reshape.183
  274.1 6.9 %all-to-all-done.2 = bf16[8,24,512]{2,1,0:T(8,128)(2,1)S(1)} async-done(((bf16[8,24,512]{2,1,0:T(8,128)(2,1)}), bf16[8,24,512]{2,1,0:T(8,128)(2,1)S(1)}, u32[]{:S(2)}, u32[]{:S(2)}) %all-to-all-start.2) | async-done | bytes 196640 | tf_op jit(solution)/shard_map/all_to_all | solution.py:133
  281.0 2.3 convolution_bitcast_fusion
  283.3 0.9 dynamic-slice_bitcast_fusion.1
  284.3 29.9 %reduce-scatter.4.cloned.1.call-done = f32[608,192]{1,0:T(8,128)} async-done(((f32[2432,192]{1,0:T(8,128)}), f32[608,192]{1,0:T(8,128)}) %reduce-scatter.4.cloned.1.call-update) | async-done | bytes 466960
  314.1 1.3 copy.106
  315.6 5.5 %all-reduce = (f32[8,24]{1,0:T(8,128)S(1)}, f32[8,24]{1,0:T(8,128)S(1)}) all-reduce(f32[8,24]{1,0:T(8,128)S(1)} %get-tuple-element.5, f32[8,24]{1,0:T(8,128)S(1)} %get-tuple-element.4), channel_id=1, replica_groups=mesh['rq'=8,'rm'=8,'col'=4] {'col'}, use_global_device_ids=true, to_apply=%region_13.14 | all-reduce | flops 384 | bytes 3072 | tf_op jit(solution)/shard_map/psum | solution.py:146
  321.1 0.2 add_convert_fusion
  321.3 0.2 fusion.68
  321.5 11.5 %psum.23 = f32[8,24,64]{2,1,0:T(8,128)S(1)} all-reduce(f32[8,24,64]{2,1,0:T(8,128)S(1)} %bitcast.128), channel_id=1, replica_groups=mesh['rq'=8,'rm'=8,'col'=4] {'col'}, use_global_device_ids=true, to_apply=%region_14.15 | all-reduce | flops 12288 | bytes 98304 | tf_op jit(solution)/shard_map/psum | solution.py:151
  333.0 0.8 multiply_subtract_fusion
  (71 shorter events, 2.6 us)
Async XLA Ops:
  7.2 314.2 %copy-start = (bf16[608,64]{0,1:T(8,128)(2,1)S(1)}, bf16[608,64]{0,1:T(8,128)(2,1)}, u32[]{:S(2)}) copy-start(bf16[608,64]{0,1:T(8,128)(2,1)} %param.20) | copy-start | bytes 233476
  7.2 198.1 %all-gather.5.cloned.1.call-start = ((), (), s32[]{:S(2)}) async-start(), calls=%async_computation.5 | async-start | bytes 3833856 | tf_op jit(solution)/shard_map/all_gather | solution.py:116
  15.9 11.8 %copy-start.3 = (f32[8,2,2432]{2,1,0:T(2,128)S(1)}, f32[8,2,2432]{2,1,0:T(2,128)}, u32[]{:S(2)}) copy-start(f32[8,2,2432]{2,1,0:T(2,128)} %param.16) | copy-start | bytes 466948
  37.4 5.4 %copy-start.6 = (f32[3,64]{1,0:T(4,128)S(1)}, f32[3,64]{1,0:T(4,128)}, u32[]{:S(2)}) copy-start(f32[3,64]{1,0:T(4,128)} %param.21) | copy-start | bytes 2308
  44.2 35.1 %copy-start.5 = (bf16[512,38]{0,1:T(8,128)(2,1)S(1)}, bf16[512,38]{0,1:T(8,128)(2,1)}, u32[]{:S(2)}) copy-start(bf16[512,38]{0,1:T(8,128)(2,1)} %param.19) | copy-start | bytes 116740
  79.3 14.5 %copy-start.7 = (s32[8]{0:T(128)S(1)}, s32[8]{0:T(128)}, u32[]{:S(2)}) copy-start(s32[8]{0:T(128)} %param.22) | copy-start | bytes 100
  80.9 184.5 %all-to-all-start.3 = ((bf16[64,38,512]{2,1,0:T(8,128)(2,1)}), bf16[64,38,512]{2,1,0:T(8,128)(2,1)}, u32[]{:S(2)}, u32[]{:S(2)}) async-start(bf16[64,38,512]{2,1,0:T(8,128)(2,1)} %stack.11), calls=%async_computation.3 | async-start | bytes 5242880 | tf_op jit(solution)/shard_map/all_to_all | solution.py:23
  247.0 12.8 %copy-start.1 = (bf16[1664,8,64]{2,1,0:T(8,128)(2,1)S(1)}, bf16[1664,8,64]{2,1,0:T(8,128)(2,1)}, u32[]{:S(2)}) copy-start(bf16[1664,8,64]{2,1,0:T(8,128)(2,1)} %reshape_squeeze.17) | copy-start | bytes 5111812
  265.4 15.6 %all-to-all-start.2 = ((bf16[8,24,512]{2,1,0:T(8,128)(2,1)}), bf16[8,24,512]{2,1,0:T(8,128)(2,1)S(1)}, u32[]{:S(2)}, u32[]{:S(2)}) async-start(bf16[8,24,512]{2,1,0:T(8,128)(2,1)} %reshape.181), calls=%async_computation.2 | async-start | bytes 393216 | tf_op jit(solution)/shard_map/all_to_all | solution.py:133
  271.3 42.8 %reduce-scatter.4.cloned.1.call-start = ((), (), s32[]{:S(2)}) async-start(), calls=%async_computation.6 | async-start | bytes 3112960
  281.0 3.2 copy-start.8
  283.3 32.1 %copy-start.2 = (bf16[8,24,608]{2,1,0:T(8,128)(2,1)S(1)}, bf16[8,24,608]{2,1,0:T(8,128)(2,1)}, u32[]{:S(2)}) copy-start(bf16[8,24,608]{2,1,0:T(8,128)(2,1)} %param.12) | copy-start | bytes 700420
  283.3 49.7 %copy-start.4 = (f32[8,24,64]{2,1,0:T(8,128)S(1)}, f32[8,24,64]{2,1,0:T(8,128)}, u32[]{:S(2)}) copy-start(f32[8,24,64]{2,1,0:T(8,128)} %param.14) | copy-start | bytes 147460
Sparse Core Ops, SparseCore 0:
  66.2 139.0 all-gather.4
  283.4 30.6 reduce-scatter.3
